TPU v7x, 256 devices: a whole 4x4x8 slice. The times are simulated.
256 devices in a mesh: expert: 32 (over z_lo, x, core), replica: 8 (over z_hi, y).
Axes of the slice: x: 4, y: 4, z: 8 (z_hi: 2, z_lo: 4; z = z_hi * 4 + z_lo), core: 2. Of those that a mesh axis runs over, the one named last changes fastest.
Arguments:
- tokens: bfloat16 [2048, 4096], P(('expert', 'replica')), may hold values from -6 to 6
- expert_ids: int32 [2048, 8], P(('expert', 'replica')), may hold values from 0 to 31, as said below
- gate_weights: float32 [2048, 8], P(('expert', 'replica')), may hold values from 0.1 to 1
- expert_holder: int32 [32], replicated, may hold values from 0 to 31, each once
- swap_pairs: int32 [8, 2], replicated, may hold values from 0 to 31, as said below
- capacity: int32 [32], replicated, may hold values from 2 to 4, as said below
- w_gate: bfloat16 [32, 1536, 4096], P('expert', 'replica'), may hold values from -0.09375 to 0.09375
- w_up: bfloat16 [32, 1536, 4096], P('expert', 'replica'), may hold values from -0.09375 to 0.09375
- w_down: bfloat16 [32, 1536, 4096], P('expert', 'replica'), may hold values from -0.15625 to 0.15625
Outputs:
- moe_output: bfloat16 [2048, 4096], P(('expert', 'replica'))
- moved_gate: bfloat16 [32, 1536, 4096], P('expert', 'replica')
- moved_up: bfloat16 [32, 1536, 4096], P('expert', 'replica')
- moved_down: bfloat16 [32, 1536, 4096], P('expert', 'replica')
- expert_peak: float32 [32], P('expert')
Inputs may be any that keep to these rules, and one draw needn't show every extreme that they name: `expert_ids`: each token names 8 different experts; among one device's 8 tokens no expert is named more than 4 times, and one expert is named exactly 4 times by the tokens of every device. `swap_pairs`: no index appears twice; the two indices of every pair differ by 16. The expert named 4 times by every device has capacity 4. `expert_holder`: each index of the expert axis holds one expert.
All inputs are finite; a program needn't handle non-finite values.
Results may differ from a plain program's by a relative error of at most 0.014.
Values may be sent and summed in bfloat16 or wider, within the bound.
No kernel may reach another device: no remote copies, remote signals or barrier semaphores. Data moves between devices by JAX's collectives and lax.ppermute only.
A program may use at most 128 MiB of HBM per device.

v0:
```python
import jax
import jax.numpy as jnp
from jax import lax
from jax.sharding import PartitionSpec as P

TOPK = 8
CAP = 4


def pair_partner(swap_pairs, device_count):
    devices = jnp.arange(device_count, dtype=jnp.int32)
    first_dev = swap_pairs[:, 0:1]
    second_dev = swap_pairs[:, 1:2]
    offsets = jnp.where(devices[None, :] == first_dev, second_dev - first_dev, 0)
    offsets = offsets + jnp.where(devices[None, :] == second_dev, first_dev - second_dev, 0)
    return devices + jnp.sum(offsets, axis=0)


def table_lookup(values_table, positions):
    matches = positions[..., None] == jnp.arange(values_table.shape[0], dtype=jnp.int32)
    return jnp.sum(jnp.where(matches, values_table, 0), axis=-1)


def route_slots(expert_ids, holder_now, capacity):
    expert_count = holder_now.shape[0]
    flat_ids = expert_ids.reshape(-1)
    chosen = (flat_ids[:, None] == jnp.arange(expert_count, dtype=jnp.int32)[None, :]).astype(
        jnp.int32
    )
    earlier = jnp.cumsum(chosen, axis=0) - chosen
    ranking = jnp.sum(earlier * chosen, axis=1)
    slot_kept = ranking < table_lookup(capacity, flat_ids)
    target = table_lookup(holder_now, flat_ids)
    slot_ids = jnp.where(slot_kept, target * CAP + ranking, -1)
    matched = slot_ids[None, :] == jnp.arange(expert_count * CAP, dtype=jnp.int32)[:, None]
    owners = jnp.arange(flat_ids.shape[0], dtype=jnp.int32) // TOPK
    source = jnp.sum(jnp.where(matched, owners[None, :], 0), axis=1)
    filled = jnp.any(matched, axis=1)
    return (jnp.maximum(slot_ids, 0), slot_kept, source, filled)


def expert_hidden(row_block, gate_local, up_local):
    leading = row_block.shape[:-1]
    row_matrix = row_block.reshape(-1, row_block.shape[-1])
    contract = (((1,), (1,)), ((), ()))
    gate_value = lax.dot_general(
        row_matrix, gate_local, contract, preferred_element_type=jnp.float32
    )
    up_value = lax.dot_general(row_matrix, up_local, contract, preferred_element_type=jnp.float32)
    hidden = (jax.nn.silu(gate_value) * up_value).astype(jnp.bfloat16)
    return hidden.reshape(leading + (gate_local.shape[0],))


def shards(
    tokens, expert_ids, gate_weights, expert_holder, swap_pairs, capacity, w_gate, w_up, w_down
):
    experts = lax.axis_size("expert")
    replicas = lax.axis_size("replica")
    tok_rows, width = tokens.shape
    partner = pair_partner(swap_pairs, experts)
    holder_after = table_lookup(partner, expert_holder)
    spread = (
        lax.all_to_all(
            w_gate.reshape(experts, -1), "expert", split_axis=0, concat_axis=0, tiled=True
        ),
        lax.all_to_all(
            w_up.reshape(experts, -1), "expert", split_axis=0, concat_axis=0, tiled=True
        ),
        lax.all_to_all(
            w_down.reshape(experts, -1), "expert", split_axis=0, concat_axis=0, tiled=True
        ),
    )
    arranged = tuple((jnp.take(pieces, partner, axis=0) for pieces in spread))
    moved = (
        lax.all_to_all(arranged[0], "expert", split_axis=0, concat_axis=0, tiled=True),
        lax.all_to_all(arranged[1], "expert", split_axis=0, concat_axis=0, tiled=True),
        lax.all_to_all(arranged[2], "expert", split_axis=0, concat_axis=0, tiled=True),
    )
    moved_gate = moved[0].reshape(w_gate.shape)
    moved_up = moved[1].reshape(w_up.shape)
    moved_down = moved[2].reshape(w_down.shape)
    gate_local, up_local, down_local = (moved_gate[0], moved_up[0], moved_down[0])
    group_tokens, group_ids = (
        lax.all_gather(tokens, "replica", axis=0, tiled=True),
        lax.all_gather(expert_ids, "replica", axis=0, tiled=True),
    )
    group_ids = group_ids.reshape(replicas, tok_rows, TOPK)
    slot_all, kept_all, source_all, filled_all = jax.vmap(route_slots, in_axes=(0, None, None))(
        group_ids, holder_after, capacity
    )
    starts = jnp.arange(replicas, dtype=jnp.int32)[:, None] * tok_rows
    picked = jnp.take(group_tokens, source_all + starts, axis=0)
    outgoing = jnp.where(filled_all[:, :, None], picked, jnp.zeros((), jnp.bfloat16))
    hidden = expert_hidden(
        lax.all_to_all(
            outgoing.reshape(replicas, experts, CAP, width),
            "expert",
            split_axis=1,
            concat_axis=1,
            tiled=True,
        ),
        gate_local,
        up_local,
    )
    replica_index = lax.axis_index("replica")
    slot_of = lax.dynamic_index_in_dim(slot_all, replica_index, 0, keepdims=False)
    slot_kept = lax.dynamic_index_in_dim(kept_all, replica_index, 0, keepdims=False)
    hidden_rows = hidden.reshape(-1, hidden.shape[-1])
    local_peak = jnp.max(jnp.abs(hidden_rows)).astype(jnp.float32)
    summed = lax.psum_scatter(
        jnp.dot(hidden_rows, down_local, preferred_element_type=jnp.float32).astype(jnp.bfloat16),
        "replica",
        scatter_dimension=0,
        tiled=True,
    )
    results = summed.reshape(experts, CAP, width)
    returned = lax.all_to_all(results, "expert", split_axis=0, concat_axis=0, tiled=True)
    fetched = jnp.take(returned.reshape(experts * CAP, width), slot_of, axis=0).reshape(
        tok_rows, TOPK, width
    )
    scales = jnp.where(slot_kept, gate_weights.reshape(-1), jnp.float32(0.0)).reshape(
        tok_rows, TOPK, 1
    )
    moe_output = jnp.sum(scales * fetched, axis=1).astype(jnp.bfloat16)
    expert_peak = lax.pmax(local_peak, "replica")
    return (moe_output, moved_gate, moved_up, moved_down, expert_peak.reshape(1))


def solution(mesh):
    placed = (
        P(("expert", "replica"), None),
        P(("expert", "replica"), None),
        P(("expert", "replica"), None),
        P(),
        P(),
        P(),
        P("expert", "replica", None),
        P("expert", "replica", None),
        P("expert", "replica", None),
    )
    return jax.shard_map(
        shards,
        mesh=mesh,
        in_specs=placed,
        out_specs=(
            P(("expert", "replica"), None),
            P("expert", "replica", None),
            P("expert", "replica", None),
            P("expert", "replica", None),
            P("expert"),
        ),
        check_vma=False,
    )
```

profile of v0, /device:TPU:2, one launch (start us, length us, event | category | flops | bytes accessed | tf_op | source)
XLA Modules:
  0.0 886.4 jit_solution(17751766660079716728)
XLA Ops:
  7.2 5.4 all_to_all.65
  13.0 11.4 %reduce.13 = bf16[32,24576]{1,0:T(8,128)(2,1)} reduce(bf16[32,1,24576]{2,1,0:T(2,128)(2,1)S(1)} %all_to_all.65, bf16[]{:T(256)} %broadcast.166), dimensions={1}, to_apply=%all_to_all.65.reduce_sub_computation | reduce | bytes 3145730 | tf_op jit(solution)/shard_map/all_to_all | solution.py:63
  24.5 3.2 reshape.259
  27.6 9.5 %all-to-all-start.1 = ((bf16[32,2,12288]{2,1,0:T(2,128)(2,1)}), bf16[32,2,12288]{2,1,0:T(2,128)(2,1)}, u32[]{:S(2)}, u32[]{:S(2)}) async-start(bf16[32,2,12288]{2,1,0:T(2,128)(2,1)} %reshape.259), calls=%async_computation.1 | async-start | bytes 3145728 | tf_op jit(solution)/shard_map/all_to_all | solution.py:63
  37.1 5.4 all_to_all.66
  42.5 11.4 %reduce.12 = bf16[32,24576]{1,0:T(8,128)(2,1)} reduce(bf16[32,1,24576]{2,1,0:T(2,128)(2,1)S(1)} %all_to_all.66, bf16[]{:T(256)} %broadcast.166), dimensions={1}, to_apply=%all_to_all.66.reduce_sub_computation | reduce | bytes 3145730 | tf_op jit(solution)/shard_map/all_to_all | solution.py:66
  53.9 3.2 reshape.255
  57.1 17.1 %all-to-all-done.1 = bf16[32,2,12288]{2,1,0:T(2,128)(2,1)} async-done(((bf16[32,2,12288]{2,1,0:T(2,128)(2,1)}), bf16[32,2,12288]{2,1,0:T(2,128)(2,1)}, u32[]{:S(2)}, u32[]{:S(2)}) %all-to-all-start.1) | async-done | bytes 1572896 | tf_op jit(solution)/shard_map/all_to_all | solution.py:63
  74.2 6.5 all-to-all-start.3
  80.7 5.4 all_to_all.67
  86.1 11.4 %reduce.11 = bf16[32,24576]{1,0:T(8,128)(2,1)} reduce(bf16[32,1,24576]{2,1,0:T(2,128)(2,1)S(1)} %all_to_all.67, bf16[]{:T(256)} %broadcast.166), dimensions={1}, to_apply=%all_to_all.67.reduce_sub_computation | reduce | bytes 3145730 | tf_op jit(solution)/shard_map/all_to_all | solution.py:69
  97.5 3.2 reshape.263
  100.7 17.1 %all-to-all-done.3 = bf16[32,2,12288]{2,1,0:T(2,128)(2,1)} async-done(((bf16[32,2,12288]{2,1,0:T(2,128)(2,1)}), bf16[32,2,12288]{2,1,0:T(2,128)(2,1)}, u32[]{:S(2)}, u32[]{:S(2)}) %all-to-all-start.3) | async-done | bytes 1572896 | tf_op jit(solution)/shard_map/all_to_all | solution.py:66
  117.7 6.3 all-to-all-start.5
  124.2 9.5 %reshape.260 = bf16[32,1,24576]{2,1,0:T(2,128)(2,1)} reshape(bf16[32,2,12288]{2,1,0:T(2,128)(2,1)} %all-to-all-done.1) | data formatting | bytes 3145728
  133.7 3.6 copy.84
  137.3 9.5 %reshape.256 = bf16[32,1,24576]{2,1,0:T(2,128)(2,1)} reshape(bf16[32,2,12288]{2,1,0:T(2,128)(2,1)} %all-to-all-done.3) | data formatting | bytes 3145728
  146.8 3.6 copy.83
  150.4 2.7 gather_fusion.2
  153.1 2.7 gather_fusion.3
  155.8 5.2 all-to-all-done.5
  161.1 9.5 %reshape.264 = bf16[32,1,24576]{2,1,0:T(2,128)(2,1)} reshape(bf16[32,2,12288]{2,1,0:T(2,128)(2,1)} %all-to-all-done.5) | data formatting | bytes 3145728
  170.6 3.6 copy.82
  174.2 2.7 gather_fusion.4
  176.9 4.0 select_bitcast_fusion
  180.8 3.9 reduce.15
  184.8 3.4 reshape.261
  188.1 6.0 all-to-all-start.2
  194.1 2.5 reduce.14
  196.6 3.2 reshape.257
  199.8 31.5 %all-to-all-done.2 = bf16[32,2,12288]{2,1,0:T(2,128)(2,1)} async-done(((bf16[32,2,12288]{2,1,0:T(2,128)(2,1)}), bf16[32,2,12288]{2,1,0:T(2,128)(2,1)}, u32[]{:S(2)}, u32[]{:S(2)}) %all-to-all-start.2) | async-done | bytes 1572896 | tf_op jit(solution)/shard_map/all_to_all | solution.py:75
  231.3 5.9 all-to-all-start.4
  237.2 67.2 %all_gather.6 = s32[64,8]{1,0:T(8,128)S(1)} all-gather(s32[8,8]{1,0:T(8,128)S(1)} %copy-done.5), channel_id=1, replica_groups=mesh['expert'=32,'replica'=8] {'replica'}, dimensions={0}, use_global_device_ids=true | all-gather | bytes 2304 | tf_op jit(solution)/shard_map/all_gather | solution.py:85
  306.2 2.5 reduce.16
  308.7 3.2 reshape.265
  311.9 7.9 all-to-all-start.6
  319.8 2.3 select_reduce_fusion.1
  322.6 60.6 %all_gather.7 = bf16[64,4096]{1,0:T(8,128)(2,1)S(1)} all-gather(bf16[8,4096]{1,0:T(8,128)(2,1)S(1)} %copy-done.4), channel_id=1, replica_groups=mesh['expert'=32,'replica'=8] {'replica'}, dimensions={0}, use_global_device_ids=true | all-gather | bytes 589824 | tf_op jit(solution)/shard_map/all_gather | solution.py:84
  383.2 7.8 gather_fusion
  391.0 13.1 %gather.16 = bf16[8,32,4,4096]{3,2,1,0:T(4,128)(2,1)} reshape(bf16[1024,4096]{1,0:T(8,128)(2,1)} %gather_fusion) | data formatting | bytes 16777216 | tf_op jit(solution)/shard_map/jit(_take)/gather | solution.py:92
  405.0 8.6 fusion
  413.6 8.3 all-to-all-start
  422.0 9.9 %reshape.262 = bf16[32,1,24576]{2,1,0:T(2,128)(2,1)} reshape(bf16[32,2,12288]{2,1,0:T(2,128)(2,1)} %all-to-all-done.2) | data formatting | bytes 3145728
  431.9 11.2 %reduce.2 = bf16[32,24576]{1,0:T(8,128)(2,1)S(1)} reduce(bf16[32,1,24576]{2,1,0:T(2,128)(2,1)} %reshape.262, bf16[]{:T(256)} %constant.99), dimensions={1}, to_apply=%all_to_all.53.reduce_sub_computation | reduce | bytes 3145730 | tf_op jit(solution)/shard_map/all_to_all | solution.py:75
  443.1 2.7 squeeze_reshape.9
  445.8 4.1 reshape.258
  449.9 11.2 %reduce.3 = bf16[32,24576]{1,0:T(8,128)(2,1)S(1)} reduce(bf16[32,1,24576]{2,1,0:T(2,128)(2,1)} %reshape.258, bf16[]{:T(256)} %constant.99), dimensions={1}, to_apply=%all_to_all.58.reduce_sub_computation | reduce | bytes 3145730 | tf_op jit(solution)/shard_map/all_to_all | solution.py:76
  461.1 2.7 squeeze_reshape.10
  463.8 9.7 %reshape.266 = bf16[32,1,24576]{2,1,0:T(2,128)(2,1)} reshape(bf16[32,2,12288]{2,1,0:T(2,128)(2,1)} %all-to-all-done.6) | data formatting | bytes 3145728
  473.5 12.3 %reduce.4 = bf16[32,24576]{1,0:T(8,128)(2,1)} reduce(bf16[32,1,24576]{2,1,0:T(2,128)(2,1)} %reshape.266, bf16[]{:T(256)} %constant.99), dimensions={1}, to_apply=%all_to_all.63.reduce_sub_computation | reduce | bytes 3145730 | tf_op jit(solution)/shard_map/all_to_all | solution.py:77
  485.8 3.9 squeeze_reshape.11
  489.6 115.8 %all-to-all-done = bf16[8,32,4,4096]{3,2,0,1:T(4,128)(2,1)} async-done(((bf16[8,32,4,4096]{3,2,0,1:T(4,128)(2,1)}), bf16[8,32,4,4096]{3,2,0,1:T(4,128)(2,1)}, u32[]{:S(2)}, u32[]{:S(2)}) %all-to-all-start) | async-done | bytes 8388640 | tf_op jit(solution)/shard_map/all_to_all | solution.py:95
  605.5 8.5 copy.66
  614.0 12.7 %reshape.188 = bf16[1024,4096]{1,0:T(8,128)(2,1)} reshape(bf16[8,32,4,4096]{3,2,1,0:T(4,128)(2,1)} %copy.66) | data formatting | bytes 16777216 | tf_op jit(solution)/shard_map/reshape | solution.py:44
  626.7 6.8 fusion.11
  633.6 3.6 abs_reduce_fusion
  637.2 5.6 convolution_convert_fusion
  642.8 184.3 %reduce-scatter.2.cloned.1.call-done = bf16[128,4096]{1,0:T(8,128)(2,1)} async-done(((bf16[1024,4096]{1,0:T(8,128)(2,1)}), bf16[128,4096]{1,0:T(8,128)(2,1)}) %reduce-scatter.2.cloned.1.call-update) | async-done | bytes 1048592 | tf_op jit(solution)/shard_map/reduce_scatter | solution.py:110
  827.1 2.3 reshape.189
  829.4 7.0 all-to-all-start.7
  837.0 2.7 reshape.191
  839.7 2.7 reshape.192
  842.4 2.7 reshape.193
  845.1 30.6 %pmax.7 = f32[1]{0:T(128)} all-reduce(bf16[1]{0:T(256)(128)(2,1)} %bitcast.14), channel_id=1, replica_groups=mesh['expert'=32,'replica'=8] {'replica'}, use_global_device_ids=true, to_apply=%region_11.13 | all-reduce | flops 1 | bytes 6 | tf_op jit(solution)/shard_map/pmax | solution.py:125
  (59 shorter events, 7.6 us)
Async XLA Ops:
  27.6 46.5 %all-to-all-start.1 = ((bf16[32,2,12288]{2,1,0:T(2,128)(2,1)}), bf16[32,2,12288]{2,1,0:T(2,128)(2,1)}, u32[]{:S(2)}, u32[]{:S(2)}) async-start(bf16[32,2,12288]{2,1,0:T(2,128)(2,1)} %reshape.259), calls=%async_computation.1 | async-start | bytes 3145728 | tf_op jit(solution)/shard_map/all_to_all | solution.py:63
  74.2 43.6 %all-to-all-start.3 = ((bf16[32,2,12288]{2,1,0:T(2,128)(2,1)}), bf16[32,2,12288]{2,1,0:T(2,128)(2,1)}, u32[]{:S(2)}, u32[]{:S(2)}) async-start(bf16[32,2,12288]{2,1,0:T(2,128)(2,1)} %reshape.255), calls=%async_computation.3 | async-start | bytes 3145728 | tf_op jit(solution)/shard_map/all_to_all | solution.py:66
  100.7 23.4 %copy-start.7 = (s32[8,2]{0,1:T(2,128)S(1)}, s32[8,2]{0,1:T(2,128)}, u32[]{:S(2)}) copy-start(s32[8,2]{0,1:T(2,128)} %param.15) | copy-start | bytes 196
  117.7 43.3 %all-to-all-start.5 = ((bf16[32,2,12288]{2,1,0:T(2,128)(2,1)}), bf16[32,2,12288]{2,1,0:T(2,128)(2,1)}, u32[]{:S(2)}, u32[]{:S(2)}) async-start(bf16[32,2,12288]{2,1,0:T(2,128)(2,1)} %reshape.263), calls=%async_computation.5 | async-start | bytes 3145728 | tf_op jit(solution)/shard_map/all_to_all | solution.py:69
  188.1 43.2 %all-to-all-start.2 = ((bf16[32,2,12288]{2,1,0:T(2,128)(2,1)}), bf16[32,2,12288]{2,1,0:T(2,128)(2,1)}, u32[]{:S(2)}, u32[]{:S(2)}) async-start(bf16[32,2,12288]{2,1,0:T(2,128)(2,1)} %reshape.261), calls=%async_computation.2 | async-start | bytes 3145728 | tf_op jit(solution)/shard_map/all_to_all | solution.py:75
  199.8 37.4 %copy-start.5 = (s32[8,8]{1,0:T(8,128)S(1)}, s32[8,8]{1,0:T(8,128)}, u32[]{:S(2)}) copy-start(s32[8,8]{1,0:T(8,128)} %param.12) | copy-start | bytes 772
  199.8 104.9 %copy-start.9 = (s32[32]{0:T(128)S(1)}, s32[32]{0:T(128)}, u32[]{:S(2)}) copy-start(s32[32]{0:T(128)} %param.14) | copy-start | bytes 388
  231.3 80.6 %all-to-all-start.4 = ((bf16[32,2,12288]{2,1,0:T(2,128)(2,1)}), bf16[32,2,12288]{2,1,0:T(2,128)(2,1)S(1)}, u32[]{:S(2)}, u32[]{:S(2)}) async-start(bf16[32,2,12288]{2,1,0:T(2,128)(2,1)} %reshape.257), calls=%async_computation.4 | async-start | bytes 3145728 | tf_op jit(solution)/shard_map/all_to_all | solution.py:76
  311.9 7.9 copy-start.8
  311.9 10.7 %copy-start.4 = (bf16[8,4096]{1,0:T(8,128)(2,1)S(1)}, bf16[8,4096]{1,0:T(8,128)(2,1)}, u32[]{:S(2)}) copy-start(bf16[8,4096]{1,0:T(8,128)(2,1)} %param.11) | copy-start | bytes 196612
  311.9 101.7 %all-to-all-start.6 = ((bf16[32,2,12288]{2,1,0:T(2,128)(2,1)}), bf16[32,2,12288]{2,1,0:T(2,128)(2,1)}, u32[]{:S(2)}, u32[]{:S(2)}) async-start(bf16[32,2,12288]{2,1,0:T(2,128)(2,1)} %reshape.265), calls=%async_computation.6 | async-start | bytes 3145728 | tf_op jit(solution)/shard_map/all_to_all | solution.py:77
  413.6 191.8 %all-to-all-start = ((bf16[8,32,4,4096]{3,2,0,1:T(4,128)(2,1)}), bf16[8,32,4,4096]{3,2,0,1:T(4,128)(2,1)}, u32[]{:S(2)}, u32[]{:S(2)}) async-start(bf16[8,32,4,4096]{3,2,0,1:T(4,128)(2,1)} %fusion), calls=%async_computation | async-start | bytes 16777216 | tf_op jit(solution)/shard_map/all_to_all | solution.py:95
  421.9 405.2 %reduce-scatter.2.cloned.1.call-start = ((), (), s32[]{:S(2)}) async-start(), calls=%async_computation.9 | async-start | bytes 9437184 | tf_op jit(solution)/shard_map/reduce_scatter | solution.py:110
  626.7 6.9 copy-start.1
  626.7 6.9 copy-start.3
  633.6 3.6 copy-start.2
  829.4 7.6 copy-start.6
  829.4 46.4 %all-to-all-start.7 = ((bf16[32,4,4096]{2,1,0:T(4,128)(2,1)}), bf16[32,4,4096]{2,1,0:T(4,128)(2,1)}, u32[]{:S(2)}, u32[]{:S(2)}) async-start(bf16[32,4,4096]{2,1,0:T(4,128)(2,1)} %reshape.189), calls=%async_computation.8 | async-start | bytes 2097152 | tf_op jit(solution)/shard_map/all_to_all | solution.py:117
  839.7 2.7 copy-start
Sparse Core Ops, SparseCore 0:
  643.0 184.1 reduce-scatter.1
where the time goes:
time: 898 us; the launch traced here: 886 us
  waiting for transfers between devices  371 us (41%)
  local copies, waits for them, and re-layouts  172 us (19%)
  blocking collectives  159 us (18%)
  other arithmetic  96.1 us (11%)
  starting transfers between devices  57.5 us (6%)
  matrix products  16 us (2%)
  between operations  14.8 us (2%)
    reduce_scatter x1, waiting for transfers between devices, shards(): lax.psum_scatter(jnp.dot(hidden_rows, down_local, preferred_element_type=...  184 us
    all_to_all x1, waiting for transfers between devices, shards(): lax.all_to_all(outgoing.reshape(replicas, experts, CAP, width), 'expert',...  116 us
    unnamed x35, local copies, waits for them, and re-layouts  82.2 us
    all_gather x1, blocking collectives, shards(): lax.all_gather(expert_ids, 'replica', axis=0, tiled=True)  67.2 us
    all_gather x1, blocking collectives, shards(): lax.all_gather(tokens, 'replica', axis=0, tiled=True)  60.6 us
    all_to_all x1, waiting for transfers between devices, shards(): lax.all_to_all(arranged[0], 'expert', split_axis=0, concat_axis=0, tiled=...  31.5 us
    pmax x1, blocking collectives, shards(): expert_peak = lax.pmax(local_peak, 'replica')  30.6 us
    gather x2, local copies, waits for them, and re-layouts, shards(): picked = jnp.take(group_tokens, source_all + starts, axis=0)  20.9 us
  transfers between devices with their start and end apart: 9, of which 6 were waited for; matrix products, arithmetic and copies ran while one was open for 21% of the time, Pallas kernels for 0%

commit v1 on v0

--- a/solution.py
+++ b/solution.py
@@ -1,3 +1,4 @@
+import functools
 import jax
 import jax.numpy as jnp
 from jax import lax
@@ -5,6 +6,22 @@
 
 TOPK = 8
 CAP = 4
+
+
+def column_search(q_in, peer_axis):
+    a_now = jnp.concatenate(
+        lax.all_to_all(
+            jnp.stack(tuple((q_in for _ in range(lax.axis_size(peer_axis)))), axis=0),
+            axis_name=peer_axis,
+            split_axis=0,
+            concat_axis=0,
+        ),
+        0,
+    )
+    return a_now
+
+
+handle_sides = functools.partial(column_search, peer_axis="replica")
 
 
 def pair_partner(swap_pairs, device_count):
@@ -82,7 +99,7 @@
     gate_local, up_local, down_local = (moved_gate[0], moved_up[0], moved_down[0])
     group_tokens, group_ids = (
         lax.all_gather(tokens, "replica", axis=0, tiled=True),
-        lax.all_gather(expert_ids, "replica", axis=0, tiled=True),
+        handle_sides(expert_ids),
     )
     group_ids = group_ids.reshape(replicas, tok_rows, TOPK)
     slot_all, kept_all, source_all, filled_all = jax.vmap(route_slots, in_axes=(0, None, None))(

time: 898 us -> 874 us (0.973)
  blocking collectives: 159 us -> 102 us
  waiting for transfers between devices: 371 us -> 396 us
    all_gather x1 -> x0, blocking collectives: 67.2 us -> none  [shards(): lax.all_gather(expert_ids, 'replica', axis=0, tiled=True)]
    all_to_all x1, waiting for transfers between devices: 0.01 us -> 31.2 us  [shards(): lax.all_to_all(arranged[1], 'expert', split_axis=0, concat_axis=0, tiled=...]
    all_gather x1, blocking collectives: 60.6 us -> 71.2 us  [shards(): lax.all_gather(tokens, 'replica', axis=0, tiled=True)]
  transfers between devices with their start and end apart: 9 -> 10, of which waited for: 6 -> 7; matrix products, arithmetic and copies ran while one was open for 21% -> 24% of each run, Pallas kernels for 0% -> 0%
where the time goes in v1:
time: 874 us; the launch traced here: 862 us
  waiting for transfers between devices  396 us (45%)
  local copies, waits for them, and re-layouts  172 us (20%)
  blocking collectives  102 us (12%)
  other arithmetic  96.1 us (11%)
  starting transfers between devices  64.5 us (7%)
  matrix products  16 us (2%)
  between operations  14.8 us (2%)
    reduce_scatter x1, waiting for transfers between devices, shards(): lax.psum_scatter(jnp.dot(hidden_rows, down_local, preferred_element_type=...  178 us
    all_to_all x1, waiting for transfers between devices, shards(): lax.all_to_all(outgoing.reshape(replicas, experts, CAP, width), 'expert',...  116 us
    unnamed x35, local copies, waits for them, and re-layouts  81.6 us
    all_gather x1, blocking collectives, shards(): lax.all_gather(tokens, 'replica', axis=0, tiled=True)  71.2 us
    all_to_all x1, waiting for transfers between devices, shards(): lax.all_to_all(arranged[0], 'expert', split_axis=0, concat_axis=0, tiled=...  31.5 us
    all_to_all x1, waiting for transfers between devices, shards(): lax.all_to_all(arranged[1], 'expert', split_axis=0, concat_axis=0, tiled=...  31.2 us
    pmax x1, blocking collectives, shards(): expert_peak = lax.pmax(local_peak, 'replica')  30.6 us
    gather x2, local copies, waits for them, and re-layouts, shards(): picked = jnp.take(group_tokens, source_all + starts, axis=0)  20.9 us
  transfers between devices with their start and end apart: 10, of which 7 were waited for; matrix products, arithmetic and copies ran while one was open for 24% of the time, Pallas kernels for 0%

profile of v1, /device:TPU:2, one launch (start us, length us, event | category | flops | bytes accessed | tf_op | source)
XLA Modules:
  0.0 861.9 jit_solution(7012255662546275042)
XLA Ops:
  7.2 5.4 all_to_all.69
  13.0 11.4 %reduce.13 = bf16[32,24576]{1,0:T(8,128)(2,1)} reduce(bf16[32,1,24576]{2,1,0:T(2,128)(2,1)S(1)} %all_to_all.69, bf16[]{:T(256)} %broadcast.168), dimensions={1}, to_apply=%all_to_all.69.reduce_sub_computation | reduce | bytes 3145730 | tf_op jit(solution)/shard_map/all_to_all | solution.py:80
  24.5 3.2 reshape.261
  27.6 9.5 %all-to-all-start.2 = ((bf16[32,2,12288]{2,1,0:T(2,128)(2,1)}), bf16[32,2,12288]{2,1,0:T(2,128)(2,1)}, u32[]{:S(2)}, u32[]{:S(2)}) async-start(bf16[32,2,12288]{2,1,0:T(2,128)(2,1)} %reshape.261), calls=%async_computation.2 | async-start | bytes 3145728 | tf_op jit(solution)/shard_map/all_to_all | solution.py:80
  37.1 5.4 all_to_all.70
  42.5 11.4 %reduce.12 = bf16[32,24576]{1,0:T(8,128)(2,1)} reduce(bf16[32,1,24576]{2,1,0:T(2,128)(2,1)S(1)} %all_to_all.70, bf16[]{:T(256)} %broadcast.168), dimensions={1}, to_apply=%all_to_all.70.reduce_sub_computation | reduce | bytes 3145730 | tf_op jit(solution)/shard_map/all_to_all | solution.py:83
  53.9 3.2 reshape.257
  57.1 17.1 %all-to-all-done.2 = bf16[32,2,12288]{2,1,0:T(2,128)(2,1)} async-done(((bf16[32,2,12288]{2,1,0:T(2,128)(2,1)}), bf16[32,2,12288]{2,1,0:T(2,128)(2,1)}, u32[]{:S(2)}, u32[]{:S(2)}) %all-to-all-start.2) | async-done | bytes 1572896 | tf_op jit(solution)/shard_map/all_to_all | solution.py:80
  74.2 6.5 all-to-all-start.4
  80.7 5.4 all_to_all.71
  86.1 11.4 %reduce.11 = bf16[32,24576]{1,0:T(8,128)(2,1)} reduce(bf16[32,1,24576]{2,1,0:T(2,128)(2,1)S(1)} %all_to_all.71, bf16[]{:T(256)} %broadcast.168), dimensions={1}, to_apply=%all_to_all.71.reduce_sub_computation | reduce | bytes 3145730 | tf_op jit(solution)/shard_map/all_to_all | solution.py:86
  97.5 3.2 reshape.265
  100.7 17.1 %all-to-all-done.4 = bf16[32,2,12288]{2,1,0:T(2,128)(2,1)} async-done(((bf16[32,2,12288]{2,1,0:T(2,128)(2,1)}), bf16[32,2,12288]{2,1,0:T(2,128)(2,1)}, u32[]{:S(2)}, u32[]{:S(2)}) %all-to-all-start.4) | async-done | bytes 1572896 | tf_op jit(solution)/shard_map/all_to_all | solution.py:83
  117.7 6.3 all-to-all-start.6
  124.2 9.5 %reshape.262 = bf16[32,1,24576]{2,1,0:T(2,128)(2,1)} reshape(bf16[32,2,12288]{2,1,0:T(2,128)(2,1)} %all-to-all-done.2) | data formatting | bytes 3145728
  133.7 3.6 copy.82
  137.3 9.5 %reshape.258 = bf16[32,1,24576]{2,1,0:T(2,128)(2,1)} reshape(bf16[32,2,12288]{2,1,0:T(2,128)(2,1)} %all-to-all-done.4) | data formatting | bytes 3145728
  146.8 3.6 copy.81
  150.4 2.7 gather_fusion.2
  153.1 2.7 gather_fusion.3
  155.8 5.2 all-to-all-done.6
  161.7 8.6 %all-to-all-start = ((s32[8,8,8]{2,1,0:T(8,128)}), s32[8,8,8]{2,1,0:T(8,128)S(1)}, u32[]{:S(2)}, u32[]{:S(2)}) async-start(s32[8,8,8]{2,1,0:T(8,128)} %stack.2), calls=%async_computation | async-start | bytes 65536 | tf_op jit(solution)/shard_map/all_to_all | solution.py:13
  170.3 9.5 %reshape.266 = bf16[32,1,24576]{2,1,0:T(2,128)(2,1)} reshape(bf16[32,2,12288]{2,1,0:T(2,128)(2,1)} %all-to-all-done.6) | data formatting | bytes 3145728
  179.8 3.6 copy.80
  183.4 2.7 gather_fusion.4
  186.2 4.0 select_bitcast_fusion
  190.1 3.9 reduce.15
  194.0 3.2 reshape.263
  197.2 6.0 all-to-all-start.3
  203.2 2.5 reduce.14
  205.7 3.2 reshape.259
  208.9 31.5 %all-to-all-done.3 = bf16[32,2,12288]{2,1,0:T(2,128)(2,1)} async-done(((bf16[32,2,12288]{2,1,0:T(2,128)(2,1)}), bf16[32,2,12288]{2,1,0:T(2,128)(2,1)}, u32[]{:S(2)}, u32[]{:S(2)}) %all-to-all-start.3) | async-done | bytes 1572896 | tf_op jit(solution)/shard_map/all_to_all | solution.py:92
  240.4 5.9 all-to-all-start.5
  246.5 2.5 reduce.16
  249.0 3.2 reshape.267
  252.2 31.2 %all-to-all-done.5 = bf16[32,2,12288]{2,1,0:T(2,128)(2,1)S(1)} async-done(((bf16[32,2,12288]{2,1,0:T(2,128)(2,1)}), bf16[32,2,12288]{2,1,0:T(2,128)(2,1)S(1)}, u32[]{:S(2)}, u32[]{:S(2)}) %all-to-all-start.5) | async-done | bytes 1572896 | tf_op jit(solution)/shard_map/all_to_all | solution.py:93
  283.4 6.0 all-to-all-start.7
  289.4 71.2 %all_gather.3 = bf16[64,4096]{1,0:T(8,128)(2,1)S(1)} all-gather(bf16[8,4096]{1,0:T(8,128)(2,1)S(1)} %copy-done.4), channel_id=1, replica_groups=mesh['expert'=32,'replica'=8] {'replica'}, dimensions={0}, use_global_device_ids=true | all-gather | bytes 589824 | tf_op jit(solution)/shard_map/all_gather | solution.py:101
  360.7 2.3 select_reduce_fusion.1
  364.9 7.8 gather_fusion
  372.7 13.1 %gather.16 = bf16[8,32,4,4096]{3,2,1,0:T(4,128)(2,1)} reshape(bf16[1024,4096]{1,0:T(8,128)(2,1)} %gather_fusion) | data formatting | bytes 16777216 | tf_op jit(solution)/shard_map/jit(_take)/gather | solution.py:109
  386.7 8.6 fusion
  395.2 8.2 all-to-all-start.1
  404.0 9.5 %reshape.264 = bf16[32,1,24576]{2,1,0:T(2,128)(2,1)} reshape(bf16[32,2,12288]{2,1,0:T(2,128)(2,1)} %all-to-all-done.3) | data formatting | bytes 3145728
  413.5 11.2 %reduce.2 = bf16[32,24576]{1,0:T(8,128)(2,1)S(1)} reduce(bf16[32,1,24576]{2,1,0:T(2,128)(2,1)} %reshape.264, bf16[]{:T(256)} %constant.99), dimensions={1}, to_apply=%all_to_all.57.reduce_sub_computation | reduce | bytes 3145730 | tf_op jit(solution)/shard_map/all_to_all | solution.py:92
  424.7 2.7 squeeze_reshape.9
  427.4 4.1 reshape.260
  431.5 11.2 %reduce.3 = bf16[32,24576]{1,0:T(8,128)(2,1)S(1)} reduce(bf16[32,1,24576]{2,1,0:T(2,128)(2,1)} %reshape.260, bf16[]{:T(256)} %constant.99), dimensions={1}, to_apply=%all_to_all.62.reduce_sub_computation | reduce | bytes 3145730 | tf_op jit(solution)/shard_map/all_to_all | solution.py:93
  442.7 2.7 squeeze_reshape.10
  445.4 9.7 %reshape.268 = bf16[32,1,24576]{2,1,0:T(2,128)(2,1)} reshape(bf16[32,2,12288]{2,1,0:T(2,128)(2,1)} %all-to-all-done.7) | data formatting | bytes 3145728
  455.1 12.3 %reduce.4 = bf16[32,24576]{1,0:T(8,128)(2,1)} reduce(bf16[32,1,24576]{2,1,0:T(2,128)(2,1)} %reshape.268, bf16[]{:T(256)} %constant.99), dimensions={1}, to_apply=%all_to_all.67.reduce_sub_computation | reduce | bytes 3145730 | tf_op jit(solution)/shard_map/all_to_all | solution.py:94
  467.4 3.9 squeeze_reshape.11
  471.2 115.8 %all-to-all-done.1 = bf16[8,32,4,4096]{3,2,0,1:T(4,128)(2,1)} async-done(((bf16[8,32,4,4096]{3,2,0,1:T(4,128)(2,1)}), bf16[8,32,4,4096]{3,2,0,1:T(4,128)(2,1)}, u32[]{:S(2)}, u32[]{:S(2)}) %all-to-all-start.1) | async-done | bytes 8388640 | tf_op jit(solution)/shard_map/all_to_all | solution.py:112
  587.0 8.5 copy.63
  595.5 12.7 %reshape.190 = bf16[1024,4096]{1,0:T(8,128)(2,1)} reshape(bf16[8,32,4,4096]{3,2,1,0:T(4,128)(2,1)} %copy.63) | data formatting | bytes 16777216 | tf_op jit(solution)/shard_map/reshape | solution.py:61
  608.3 6.8 fusion.11
  615.2 3.6 abs_reduce_fusion
  618.8 5.6 convolution_convert_fusion
  624.4 178.3 %reduce-scatter.2.cloned.1.call-done = bf16[128,4096]{1,0:T(8,128)(2,1)} async-done(((bf16[1024,4096]{1,0:T(8,128)(2,1)}), bf16[128,4096]{1,0:T(8,128)(2,1)}) %reduce-scatter.2.cloned.1.call-update) | async-done | bytes 1048592 | tf_op jit(solution)/shard_map/reduce_scatter | solution.py:127
  805.0 6.9 all-to-all-start.8
  812.5 2.7 reshape.193
  815.3 2.7 reshape.194
  818.0 2.7 reshape.195
  820.7 30.6 %pmax.7 = f32[1]{0:T(128)} all-reduce(bf16[1]{0:T(256)(128)(2,1)} %bitcast.15), channel_id=1, replica_groups=mesh['expert'=32,'replica'=8] {'replica'}, use_global_device_ids=true, to_apply=%region_11.13 | all-reduce | flops 1 | bytes 6 | tf_op jit(solution)/shard_map/pmax | solution.py:142
  (60 shorter events, 10.9 us)
Async XLA Ops:
  27.6 46.5 %all-to-all-start.2 = ((bf16[32,2,12288]{2,1,0:T(2,128)(2,1)}), bf16[32,2,12288]{2,1,0:T(2,128)(2,1)}, u32[]{:S(2)}, u32[]{:S(2)}) async-start(bf16[32,2,12288]{2,1,0:T(2,128)(2,1)} %reshape.261), calls=%async_computation.2 | async-start | bytes 3145728 | tf_op jit(solution)/shard_map/all_to_all | solution.py:80
  74.2 43.6 %all-to-all-start.4 = ((bf16[32,2,12288]{2,1,0:T(2,128)(2,1)}), bf16[32,2,12288]{2,1,0:T(2,128)(2,1)}, u32[]{:S(2)}, u32[]{:S(2)}) async-start(bf16[32,2,12288]{2,1,0:T(2,128)(2,1)} %reshape.257), calls=%async_computation.4 | async-start | bytes 3145728 | tf_op jit(solution)/shard_map/all_to_all | solution.py:83
  100.7 23.4 %copy-start.7 = (s32[8,2]{0,1:T(2,128)S(1)}, s32[8,2]{0,1:T(2,128)}, u32[]{:S(2)}) copy-start(s32[8,2]{0,1:T(2,128)} %param.15) | copy-start | bytes 196
  117.7 43.3 %all-to-all-start.6 = ((bf16[32,2,12288]{2,1,0:T(2,128)(2,1)}), bf16[32,2,12288]{2,1,0:T(2,128)(2,1)}, u32[]{:S(2)}, u32[]{:S(2)}) async-start(bf16[32,2,12288]{2,1,0:T(2,128)(2,1)} %reshape.265), calls=%async_computation.6 | async-start | bytes 3145728 | tf_op jit(solution)/shard_map/all_to_all | solution.py:86
  153.1 7.9 copy-start.5
  161.7 35.5 %all-to-all-start = ((s32[8,8,8]{2,1,0:T(8,128)}), s32[8,8,8]{2,1,0:T(8,128)S(1)}, u32[]{:S(2)}, u32[]{:S(2)}) async-start(s32[8,8,8]{2,1,0:T(8,128)} %stack.2), calls=%async_computation | async-start | bytes 65536 | tf_op jit(solution)/shard_map/all_to_all | solution.py:13
  197.2 43.2 %all-to-all-start.3 = ((bf16[32,2,12288]{2,1,0:T(2,128)(2,1)}), bf16[32,2,12288]{2,1,0:T(2,128)(2,1)}, u32[]{:S(2)}, u32[]{:S(2)}) async-start(bf16[32,2,12288]{2,1,0:T(2,128)(2,1)} %reshape.263), calls=%async_computation.3 | async-start | bytes 3145728 | tf_op jit(solution)/shard_map/all_to_all | solution.py:92
  208.9 37.5 %copy-start.9 = (s32[32]{0:T(128)S(1)}, s32[32]{0:T(128)}, u32[]{:S(2)}) copy-start(s32[32]{0:T(128)} %param.14) | copy-start | bytes 388
  240.4 43.1 %all-to-all-start.5 = ((bf16[32,2,12288]{2,1,0:T(2,128)(2,1)}), bf16[32,2,12288]{2,1,0:T(2,128)(2,1)S(1)}, u32[]{:S(2)}, u32[]{:S(2)}) async-start(bf16[32,2,12288]{2,1,0:T(2,128)(2,1)} %reshape.259), calls=%async_computation.5 | async-start | bytes 3145728 | tf_op jit(solution)/shard_map/all_to_all | solution.py:93
  252.2 37.2 %copy-start.4 = (bf16[8,4096]{1,0:T(8,128)(2,1)S(1)}, bf16[8,4096]{1,0:T(8,128)(2,1)}, u32[]{:S(2)}) copy-start(bf16[8,4096]{1,0:T(8,128)(2,1)} %param.11) | copy-start | bytes 196612
  252.2 108.5 %copy-start.8 = (s32[32]{0:T(128)S(1)}, s32[32]{0:T(128)}, u32[]{:S(2)}) copy-start(s32[32]{0:T(128)} %param.16) | copy-start | bytes 388
  283.4 111.8 %all-to-all-start.7 = ((bf16[32,2,12288]{2,1,0:T(2,128)(2,1)}), bf16[32,2,12288]{2,1,0:T(2,128)(2,1)}, u32[]{:S(2)}, u32[]{:S(2)}) async-start(bf16[32,2,12288]{2,1,0:T(2,128)(2,1)} %reshape.267), calls=%async_computation.7 | async-start | bytes 3145728 | tf_op jit(solution)/shard_map/all_to_all | solution.py:94
  395.2 191.8 %all-to-all-start.1 = ((bf16[8,32,4,4096]{3,2,0,1:T(4,128)(2,1)}), bf16[8,32,4,4096]{3,2,0,1:T(4,128)(2,1)}, u32[]{:S(2)}, u32[]{:S(2)}) async-start(bf16[8,32,4,4096]{3,2,0,1:T(4,128)(2,1)} %fusion), calls=%async_computation.1 | async-start | bytes 16777216 | tf_op jit(solution)/shard_map/all_to_all | solution.py:112
  403.5 399.2 %reduce-scatter.2.cloned.1.call-start = ((), (), s32[]{:S(2)}) async-start(), calls=%async_computation.10 | async-start | bytes 9437184 | tf_op jit(solution)/shard_map/reduce_scatter | solution.py:127
  608.3 6.9 copy-start.1
  608.3 6.9 copy-start.3
  615.2 3.6 copy-start.2
  805.0 7.5 copy-start.6
  805.0 46.4 %all-to-all-start.8 = ((bf16[32,4,4096]{2,1,0:T(4,128)(2,1)}), bf16[32,4,4096]{2,1,0:T(4,128)(2,1)}, u32[]{:S(2)}, u32[]{:S(2)}) async-start(bf16[32,4,4096]{2,1,0:T(4,128)(2,1)} %reshape.191), calls=%async_computation.9 | async-start | bytes 2097152 | tf_op jit(solution)/shard_map/all_to_all | solution.py:134
  815.3 2.7 copy-start
Sparse Core Ops, SparseCore 0:
  624.5 178.1 reduce-scatter.1
